TPU v7x, 256 devices: a whole 4x4x8 slice. The times are simulated.
256 devices in a mesh: row: 8 (over y, core), col: 32 (over x, z).
Axes of the slice: x: 4, y: 4, z: 8, core: 2. Of those that a mesh axis runs over, the one named last changes fastest.
Arguments:
- hidden: bfloat16 [32768, 4608], P('col', 'row'), may hold values from -6 to 6
- w_query: bfloat16 [4608, 4096], P('col', 'row'), may hold values from -0.09375 to 0.09375
- w_key: bfloat16 [4608, 2048], P('col', 'row'), may hold values from -0.09375 to 0.09375
- w_value: bfloat16 [4608, 2048], P('col', 'row'), may hold values from -0.09375 to 0.09375
- adapter_down: bfloat16 [32, 4608, 32], P('col', 'row'), may hold values from -0.09375 to 0.09375
- adapter_up_query: bfloat16 [32, 16, 4096], P('col', None, 'row'), may hold values from -1.5 to 1.5
- adapter_up_value: bfloat16 [32, 16, 2048], P('col', None, 'row'), may hold values from -1.5 to 1.5
- lengths: int32 [32, 10], P('col'), may hold values from 1 to 192, 1024 in all within a row
- request_adapter: int32 [32, 10], P('col'), may hold values from 0 to 31
- adapter_slot: int32 [32], replicated, may hold values from 0 to 31, each once
- page_table: int32 [32, 18], P('col'), may hold values from 0 to 17, each once within a row
Outputs:
- query: bfloat16 [32768, 4096], P('col', 'row')
- key_cache: bfloat16 [576, 128, 2048], P('col', None, 'row')
- value_cache: bfloat16 [576, 128, 2048], P('col', None, 'row')
Inputs may be any that keep to these rules, and one draw needn't show every extreme that they name: Each row of lengths sums to 1024, and its longest request has exactly 192 tokens. `adapter_slot`: a permutation of the slots. `page_table`: each row is a permutation of the 18 local slots.
All inputs are finite; a program needn't handle non-finite values.
Results may differ from a plain program's by a relative error of at most 0.0039.
Values may be sent and summed in bfloat16 or wider, within the bound.
No kernel may reach another device: no remote copies, remote signals or barrier semaphores. Data moves between devices by JAX's collectives and lax.ppermute only.
A program may use at most 128 MiB of HBM per device.

v0:
```python
import math
import jax
import jax.numpy as jnp
from jax import lax
from jax.sharding import PartitionSpec as P

HEAD = 128
PAGE = 128
TOK_DEV = 1024


def rotate(values, cosine, sine_value):
    half_width = HEAD // 2
    shaped = values.reshape(values.shape[0], -1, HEAD)
    leading = shaped[:, :, :half_width]
    second = shaped[:, :, half_width:]
    rotated = jnp.concatenate(
        [leading * cosine - second * sine_value, second * cosine + leading * sine_value], axis=2
    )
    return rotated.reshape(values.shape)


def token_layout(lengths, chosen_request):
    token_index = jnp.arange(TOK_DEV, dtype=jnp.int32)
    starts = jnp.cumsum(lengths) - lengths
    inside = (token_index[:, None] >= starts[None, :]) & (
        token_index[:, None] < (starts + lengths)[None, :]
    )
    inside = inside.astype(jnp.int32)
    position = token_index - jnp.sum(inside * starts[None, :], axis=1)
    chosen = jnp.sum(inside * chosen_request[None, :], axis=1)
    return (starts, position, chosen)


def cache_rows(lengths, starts, page_row):
    pages = page_row.shape[0]
    pages_each = (lengths + PAGE - 1) // PAGE
    page_start = jnp.cumsum(pages_each) - pages_each
    page_ids = jnp.arange(pages, dtype=jnp.int32)
    owner = (page_row[:, None] == page_ids[None, :]).astype(jnp.int32)
    page_of_slot = jnp.sum(owner * page_ids[:, None], axis=0)
    member = (page_of_slot[:, None] >= page_start[None, :]) & (
        page_of_slot[:, None] < (page_start + pages_each)[None, :]
    )
    member = member.astype(jnp.int32)
    used = jnp.sum(member, axis=1) > 0
    first_page = jnp.sum(member * page_start[None, :], axis=1)
    first_token = jnp.sum(member * starts[None, :], axis=1)
    length = jnp.sum(member * lengths[None, :], axis=1)
    offset = (page_of_slot - first_page) * PAGE
    source = first_token + offset
    valid = jnp.where(used, jnp.minimum(length - offset, PAGE), 0)
    inner = jnp.arange(PAGE, dtype=jnp.int32)
    rows = (source[:, None] + inner[None, :]).reshape(-1)
    keep = (inner[None, :] < valid[:, None]).reshape(-1)
    rows = jnp.clip(rows, 0, TOK_DEV - 1)
    return (rows, keep)


def shards(
    hidden,
    w_query,
    w_key,
    w_value,
    adapter_down,
    adapter_up_query,
    adapter_up_value,
    lengths,
    request_adapter,
    adapter_slot,
    page_table,
):
    lengths = lengths[0]
    chosen_request = jnp.take(adapter_slot, request_adapter[0])
    starts, position, chosen = token_layout(lengths, chosen_request)
    adapter_count = adapter_slot.shape[0]
    rank_width = adapter_up_query.shape[1]
    query_width = w_query.shape[1]
    key_width = w_key.shape[1]
    weight_width = query_width + 2 * key_width
    feature_rows = w_query.shape[0]
    down_shape = adapter_down.shape[1:]
    row_size = lax.axis_size("row")
    with jax.named_scope("gathers"):
        full_rows = lax.all_gather(hidden, "row", axis=1, tiled=True)
        pieces = [
            jnp.concatenate([w_query, w_key, w_value], axis=1),
            adapter_down.reshape(-1, weight_width),
            adapter_up_query.reshape(-1, weight_width),
            adapter_up_value.reshape(-1, weight_width),
        ]
        bounds = [0]
        for piece in pieces:
            bounds.append(bounds[-1] + piece.shape[0])
        packed = lax.all_gather(jnp.concatenate(pieces, axis=0), "col", axis=0)
        weights = packed[:, : bounds[1]].reshape(-1, weight_width)
        down_local = packed[:, bounds[1] : bounds[2]].reshape((adapter_count,) + down_shape)
        up_query = packed[:, bounds[2] : bounds[3]].reshape(adapter_count, rank_width, -1)
        up_value = packed[:, bounds[3] : bounds[4]].reshape(adapter_count, rank_width, -1)
    with jax.named_scope("lowrank"):
        onehot = chosen[:, None] == jnp.arange(adapter_count, dtype=jnp.int32)[None, :]
        partial_all = jnp.einsum(
            "tf,sfr->tsr", hidden, down_local, preferred_element_type=jnp.float32
        )
        partial = jnp.sum(jnp.where(onehot[:, :, None], partial_all, 0.0), axis=1)
        distance = 1
        while distance < row_size:
            pairs = [(i, i ^ distance) for i in range(row_size)]
            partial = partial + lax.ppermute(partial, "row", pairs)
            distance *= 2
        lowrank = partial.astype(jnp.bfloat16)
        onehot_b = onehot.astype(jnp.bfloat16)
        spread_query = (onehot_b[:, :, None] * lowrank[:, None, :rank_width]).reshape(
            -1, adapter_count * rank_width
        )
        spread_value = (onehot_b[:, :, None] * lowrank[:, None, rank_width:]).reshape(
            -1, adapter_count * rank_width
        )
        delta_query = jnp.dot(
            spread_query,
            up_query.reshape(adapter_count * rank_width, -1),
            preferred_element_type=jnp.float32,
        )
        delta_value = jnp.dot(
            spread_value,
            up_value.reshape(adapter_count * rank_width, -1),
            preferred_element_type=jnp.float32,
        )
    with jax.named_scope("projection"):
        base = jnp.dot(full_rows, weights, preferred_element_type=jnp.float32)
        base_query = base[:, :query_width]
        base_key = base[:, query_width : query_width + key_width]
        base_value = base[:, query_width + key_width :]
    with jax.named_scope("rotary"):
        half_width = HEAD // 2
        frequency = jnp.exp(
            jnp.arange(half_width, dtype=jnp.float32) * (-2.0 * math.log(10000.0) / HEAD)
        )
        angles = position.astype(jnp.float32)[:, None] * frequency[None, :]
        cosine = jnp.cos(angles)[:, None, :]
        sine_value = jnp.sin(angles)[:, None, :]
        query = rotate(base_query + delta_query, cosine, sine_value).astype(jnp.bfloat16)
        key_rotated = rotate(base_key, cosine, sine_value).astype(jnp.bfloat16)
        value_rows = (base_value + delta_value).astype(jnp.bfloat16)
    with jax.named_scope("cache_write"):
        pages = page_table.shape[1]
        rows, keep = cache_rows(lengths, starts, page_table[0])
        key_cache = jnp.where(keep[:, None], jnp.take(key_rotated, rows, axis=0), 0).reshape(
            pages, PAGE, key_width
        )
        value_cache = jnp.where(keep[:, None], jnp.take(value_rows, rows, axis=0), 0).reshape(
            pages, PAGE, key_width
        )
    return (query, key_cache.astype(jnp.bfloat16), value_cache.astype(jnp.bfloat16))


def solution(mesh):
    return jax.shard_map(
        shards,
        mesh=mesh,
        in_specs=(
            P("col", "row"),
            P("col", "row"),
            P("col", "row"),
            P("col", "row"),
            P("col", "row", None),
            P("col", None, "row"),
            P("col", None, "row"),
            P("col", None),
            P("col", None),
            P(),
            P("col", None),
        ),
        out_specs=(P("col", "row"), P("col", None, "row"), P("col", None, "row")),
        check_vma=False,
    )
```

profile of v0, /device:TPU:1, one launch (start us, length us, event | category | flops | bytes accessed | tf_op | source)
XLA Modules:
  0.0 240.4 jit_solution(12034622873768710716)
XLA Ops:
  7.3 0.7 reshape.325
  8.0 0.7 reshape.324
  8.7 0.9 copy.31
  9.8 1.8 maximum_bitcast_fusion
  11.7 0.7 all-gather.5.cloned.1.call-update
  12.8 0.7 gather_fusion
  13.8 0.7 compare_and_fusion
  14.5 0.7 fusion.10
  15.2 1.0 multiply_cosine_fusion
  16.2 112.1 %all-gather.7.cloned.1.call-done = bf16[32,174,1024]{2,1,0:T(8,128)(2,1)} async-done(((bf16[1,174,1024]{2,1,0:T(8,128)(2,1)}), bf16[32,174,1024]{2,1,0:T(8,128)(2,1)}) %all-gather.7.cloned.1.call-update) | async-done | bytes 11403280 | tf_op jit(solution)/shard_map/gathers/all_gather | solution.py:95
  128.3 1.4 slice-done.3
  129.7 4.8 %reshape.328 = bf16[32,576,32]{2,1,0:T(8,128)(2,1)} reshape(bf16[32,18,1024]{2,1,0:T(8,128)(2,1)S(1)} %slice-done.3) | data formatting | bytes 2359296 | tf_op jit(solution)/shard_map/gathers/reshape | solution.py:97
  134.6 5.6 %fusion = f32[1024,32]{0,1:T(8,128)S(1)} fusion(bf16[32,576,32]{2,1,0:T(8,128)(2,1)} %reshape.328, pred[1024,32]{0,1:T(8,128)(4,1)S(1)} %get-tuple-element.23, bf16[1024,576]{0,1:T(8,128)(2,1)S(1)} %copy-done.2), kind=kOutput, calls=%fused_computation.4 | convolution fusion | flops 1210023936 | bytes 2523136 | tf_op jit(solution)/shard_map/lowrank/tf,sfr->tsr/dot_general | solution.py:102
  140.1 1.5 collective-permute-start
  141.6 0.6 fusion.4
  142.3 9.5 %slice.58 = bf16[32,144,1024]{2,1,0:T(8,128)(2,1)} slice(bf16[32,174,1024]{2,1,0:T(8,128)(2,1)} %all-gather.7.cloned.1.call-done), slice={[0:32], [0:144], [0:1024]} | slice | bytes 18874368 | tf_op jit(solution)/shard_map/gathers/slice | solution.py:96
  151.8 1.6 collective-permute-start.1
  153.4 33.7 %all-gather.5.cloned.1.call-done = bf16[1024,4608]{0,1:T(8,128)(2,1)} async-done(((bf16[1024,576]{0,1:T(8,128)(2,1)}), bf16[1024,4608]{0,1:T(8,128)(2,1)}) %all-gather.5.cloned.1.call-update) | async-done | bytes 9437200 | tf_op jit(solution)/shard_map/gathers/all_gather | solution.py:85
  187.1 14.7 %convolution_bitcast_fusion = f32[1024,1024]{0,1:T(8,128)S(1)} fusion(bf16[4608,1024]{1,0:T(8,128)(2,1)} %bitcast.63, bf16[1024,4608]{0,1:T(8,128)(2,1)} %all-gather.5.cloned.1.call-done), kind=kOutput, calls=%fused_computation.5 | convolution fusion | flops 9663676416 | bytes 23068672 | tf_op jit(solution)/shard_map/projection/dot_general | solution.py:130
  201.9 2.7 %collective-permute-start.2 = (f32[1024,32]{0,1:T(8,128)S(1)}, f32[1024,32]{0,1:T(8,128)S(1)}, u32[]{:S(2)}, u32[]{:S(2)}) collective-permute-start(f32[1024,32]{0,1:T(8,128)S(1)} %add.98), channel_id=1, source_target_pairs={{0,128},{32,160},{64,192},{96,224},{128,0},{160,32},{192,64},{224,... | collective-permute-start | bytes 393224 | tf_op jit(solution)/shard_map/lowrank/ppermute | solution.py:109
  205.2 1.4 slice.62
  206.6 1.0 reshape.329
  207.6 0.2 copy.40
  207.8 6.9 %gather_fusion.1 = bf16[2304,256]{1,0:T(8,128)(2,1)S(1)} fusion(bf16[1024,256]{1,0:T(8,128)(2,1)S(1)} %copy.40, s32[3072]{0:T(1024)S(1)} %pad_clamp_fusion), kind=kCustom, calls=%fused_computation.clone | custom fusion | bytes 2368512 | tf_op jit(solution)/shard_map/cache_write/jit(_take)/gather | solution.py:148
  214.7 1.0 broadcast_multiply_fusion
  215.7 2.5 %fusion.1 = bf16[1024,256]{0,1:T(8,128)(2,1)} fusion(bf16[1024,512]{0,1:T(8,128)(2,1)S(1)} %bitcast.68, bf16[512,256]{1,0:T(8,128)(2,1)S(1)} %reshape.333, f32[1024,1024]{0,1:T(8,128)} %copy-done.1), kind=kOutput, calls=%fused_computation.8 | convolution fusion | flops 268959744 | bytes 2883584 | tf_op jit(solution)/shard_map/lowrank/dot_general | solution.py:124
  218.2 1.2 copy.36
  219.5 2.5 %slice_add_fusion = f32[1024,512]{0,1:T(8,128)S(1)} fusion(f32[1024,1024]{0,1:T(8,128)} %copy-done.1, bf16[1024,512]{0,1:T(8,128)(2,1)S(1)} %bitcast.67, bf16[512,512]{1,0:T(8,128)(2,1)} %reshape.329), kind=kOutput, calls=%fused_computation.6 | convolution fusion | flops 537395200 | bytes 5767168 | tf_op jit(solution)/shard_map/lowrank/dot_general | solution.py:119
  222.0 0.3 subtract_convert_fusion
  222.5 1.3 copy.39
  223.8 6.9 %gather_fusion.2 = bf16[2304,256]{1,0:T(8,128)(2,1)S(1)} fusion(bf16[1024,256]{1,0:T(8,128)(2,1)S(1)} %copy.36, s32[3072]{0:T(1024)S(1)} %pad_clamp_fusion), kind=kCustom, calls=%fused_computation.1.clone | custom fusion | bytes 2368512 | tf_op jit(solution)/shard_map/cache_write/jit(_take)/gather | solution.py:151
  230.7 2.9 %select_select_fusion = (bf16[2304,256]{1,0:T(8,128)(2,1)}, bf16[2304,256]{1,0:T(8,128)(2,1)}) fusion(bf16[2304,256]{1,0:T(8,128)(2,1)S(1)} %gather_fusion.2, pred[2304]{0:T(1024)(128)(4,1)S(1)} %copy-done.3, pred[2304]{0:T(1024)(128)(4,1)S(1)} %copy-done.4, bf16[2304,256]{1,0:T(8,128)(2,1)S(1)} %gather_fusion.1), kind=kLoop, calls=%fused_computation.10 | loop fusion | flops 2359296 | bytes 4723200 | tf_op jit(solution)/shard_map/cache_write/jit(_where)/select_n | solution.py:151
  (55 shorter events, 1.9 us)
Async XLA Ops:
  7.2 5.6 %copy-start = (s32[32]{0:T(128)S(1)}, s32[32]{0:T(128)}, u32[]{:S(2)}) copy-start(s32[32]{0:T(128)} %param.22) | copy-start | bytes 388
  7.2 5.2 %copy-start.5 = (s32[1,10]{1,0:T(1,128)S(1)}, s32[1,10]{1,0:T(1,128)}, u32[]{:S(2)}) copy-start(s32[1,10]{1,0:T(1,128)} %param.20) | copy-start | bytes 124
  7.2 5.6 %copy-start.6 = (s32[1,10]{1,0:T(1,128)S(1)}, s32[1,10]{1,0:T(1,128)}, u32[]{:S(2)}) copy-start(s32[1,10]{1,0:T(1,128)} %param.21) | copy-start | bytes 124
  7.2 6.2 %copy-start.7 = (s32[1,18]{1,0:T(1,128)S(1)}, s32[1,18]{1,0:T(1,128)}, u32[]{:S(2)}) copy-start(s32[1,18]{1,0:T(1,128)} %param.23) | copy-start | bytes 220
  7.2 121.1 %all-gather.7.cloned.1.call-start = ((), (), s32[]{:S(2)}) async-start(), calls=%async_computation.1 | async-start | bytes 11894784 | tf_op jit(solution)/shard_map/gathers/all_gather | solution.py:95
  11.6 175.5 %all-gather.5.cloned.1.call-start = ((), (), s32[]{:S(2)}) async-start(), calls=%async_computation | async-start | bytes 10616832 | tf_op jit(solution)/shard_map/gathers/all_gather | solution.py:85
  128.3 1.4 slice-start.3
  129.7 4.9 %copy-start.2 = (bf16[1024,576]{0,1:T(8,128)(2,1)S(1)}, bf16[1024,576]{0,1:T(8,128)(2,1)}, u32[]{:S(2)}) copy-start(bf16[1024,576]{0,1:T(8,128)(2,1)} %param.13) | copy-start | bytes 3538948
  140.1 11.7 %collective-permute-start = (f32[1024,32]{0,1:T(8,128)S(1)}, f32[1024,32]{0,1:T(8,128)S(1)}, u32[]{:S(2)}, u32[]{:S(2)}) collective-permute-start(f32[1024,32]{0,1:T(8,128)S(1)} %fusion), channel_id=1, source_target_pairs={{0,32},{32,0},{64,96},{96,64},{128,160},{160,128},{192,224},{224,1... | collective-permute-start | bytes 393224 | tf_op jit(solution)/shard_map/lowrank/ppermute | solution.py:109
  151.8 50.1 %collective-permute-start.1 = (f32[1024,32]{0,1:T(8,128)S(1)}, f32[1024,32]{0,1:T(8,128)S(1)}, u32[]{:S(2)}, u32[]{:S(2)}) collective-permute-start(f32[1024,32]{0,1:T(8,128)S(1)} %add.97), channel_id=1, source_target_pairs={{0,64},{32,96},{64,0},{96,32},{128,192},{160,224},{192,128},{224,1... | collective-permute-start | bytes 393224 | tf_op jit(solution)/shard_map/lowrank/ppermute | solution.py:109
  187.1 17.7 %slice-start = ((s8[11534336]{0:T(1024)(128)(4,1)}), s8[4194304]{0:T(1024)(128)(4,1)S(1)}, s32[]{:S(2)}) async-start(s8[11534336]{0:T(1024)(128)(4,1)} %bitcast.61), calls=%async_computation.2 | async-start | bytes 8388608
  187.1 17.7 %slice-start.1 = ((s8[11534336]{0:T(1024)(128)(4,1)}), s8[4194304]{0:T(1024)(128)(4,1)S(1)}, s32[]{:S(2)}) async-start(s8[11534336]{0:T(1024)(128)(4,1)} %bitcast.61), calls=%async_computation.3 | async-start | bytes 8388608
  187.1 17.8 %slice-start.2 = ((s8[11534336]{0:T(1024)(128)(4,1)}), s8[3145728]{0:T(1024)(128)(4,1)S(1)}, s32[]{:S(2)}) async-start(s8[11534336]{0:T(1024)(128)(4,1)} %bitcast.61), calls=%async_computation.4 | async-start | bytes 6291456
  201.8 3.0 %copy-start.1 = (f32[1024,1024]{0,1:T(8,128)}, f32[1024,1024]{0,1:T(8,128)S(1)}, u32[]{:S(2)}) copy-start(f32[1024,1024]{0,1:T(8,128)S(1)} %convolution_bitcast_fusion) | copy-start | bytes 12582916
  201.9 12.8 %collective-permute-start.2 = (f32[1024,32]{0,1:T(8,128)S(1)}, f32[1024,32]{0,1:T(8,128)S(1)}, u32[]{:S(2)}, u32[]{:S(2)}) collective-permute-start(f32[1024,32]{0,1:T(8,128)S(1)} %add.98), channel_id=1, source_target_pairs={{0,128},{32,160},{64,192},{96,224},{128,0},{160,32},{192,64},{224,... | collective-permute-start | bytes 393224 | tf_op jit(solution)/shard_map/lowrank/ppermute | solution.py:109
  223.8 6.9 %copy-start.3 = (pred[2304]{0:T(1024)(128)(4,1)S(1)}, pred[2304]{0:T(1024)(128)(4,1)}, u32[]{:S(2)}) copy-start(pred[2304]{0:T(1024)(128)(4,1)} %compare_and_fusion) | copy-start | bytes 6916
  223.8 6.9 %copy-start.4 = (pred[2304]{0:T(1024)(128)(4,1)S(1)}, pred[2304]{0:T(1024)(128)(4,1)}, u32[]{:S(2)}) copy-start(pred[2304]{0:T(1024)(128)(4,1)} %fusion.4) | copy-start | bytes 6916
Sparse Core Ops, SparseCore 0:
  11.7 116.5 all-gather.6
  130.1 56.9 all-gather.4
where the time goes:
time: 241 us; the launch traced here: 240 us
  waiting for transfers between devices  147 us (61%)
  local copies, waits for them, and re-layouts  38.3 us (16%)
  matrix products  25.3 us (10%)
  between operations  14.4 us (6%)
  other arithmetic  10 us (4%)
  starting transfers between devices  5.83 us (2%)
    all_gather x1, waiting for transfers between devices, shards(): packed = lax.all_gather(jnp.concatenate(pieces, axis=0), 'col', axis=0)  112 us
    all_gather x1, waiting for transfers between devices, shards(): full_rows = lax.all_gather(hidden, 'row', axis=1, tiled=True)  33.7 us
    dot_general x1, matrix products, shards(): base = jnp.dot(full_rows, weights, preferred_element_type=jnp.float32)  14.7 us
    slice x1, local copies, waits for them, and re-layouts, shards(): weights = packed[:, :bounds[1]].reshape(-1, weight_width)  9.52 us
    gather x1, local copies, waits for them, and re-layouts, shards(): jnp.take(key_rotated, rows, axis=0)  6.86 us
    gather x1, local copies, waits for them, and re-layouts, shards(): jnp.take(value_rows, rows, axis=0)  6.86 us
    ppermute x3, starting transfers between devices, shards(): partial = partial + lax.ppermute(partial, 'row', pairs)  5.75 us
    dot_general x1, matrix products, shards(): jnp.einsum('tf,sfr->tsr', hidden, down_local, preferred_element_type=jnp....  5.55 us
  transfers between devices with their start and end apart: 5, of which 2 were waited for; matrix products, arithmetic and copies ran while one was open for 20% of the time, Pallas kernels for 0%

commit v1 on v0

--- a/solution.py
+++ b/solution.py
@@ -82,7 +82,15 @@
     down_shape = adapter_down.shape[1:]
     row_size = lax.axis_size("row")
     with jax.named_scope("gathers"):
-        full_rows = lax.all_gather(hidden, "row", axis=1, tiled=True)
+        full_rows = jnp.concatenate(
+            lax.all_to_all(
+                jnp.stack([hidden for _ in range(lax.axis_size("row"))], axis=0),
+                axis_name="row",
+                split_axis=0,
+                concat_axis=0,
+            ),
+            axis=1,
+        )
         pieces = [
             jnp.concatenate([w_query, w_key, w_value], axis=1),
             adapter_down.reshape(-1, weight_width),

time: 241 us -> 206 us (0.85)
  waiting for transfers between devices: 147 us -> 99.7 us
  starting transfers between devices: 5.83 us -> 13.8 us
  local copies, waits for them, and re-layouts: 38.3 us -> 42.7 us
    all_gather x1 -> x0, waiting for transfers between devices: 33.7 us -> none  [shards(): full_rows = lax.all_gather(hidden, 'row', axis=1, tiled=True)]
    all_gather x1, waiting for transfers between devices: 112 us -> 99.7 us  [shards(): packed = lax.all_gather(jnp.concatenate(pieces, axis=0), 'col', axis=0)]
    all_to_all x0 -> x1, starting transfers between devices: none -> 8.27 us  [shards(): lax.all_to_all(jnp.stack([hidden for _ in range(lax.axis_size('row'))], a...]
    another operation x0 -> x1, local copies, waits for them, and re-layouts: none -> 4.86 us  [shards(): jnp.stack([hidden for _ in range(lax.axis_size('row'))], axis=0)]
  transfers between devices with their start and end apart: 5 -> 5, of which waited for: 2 -> 1; matrix products, arithmetic and copies ran while one was open for 20% -> 26% of each run, Pallas kernels for 0% -> 0%
where the time goes in v1:
time: 206 us
  waiting for transfers between devices  99.7 us (48%)
  local copies, waits for them, and re-layouts  42.7 us (21%)
  matrix products  25.3 us (12%)
  between operations  14.3 us (7%)
  starting transfers between devices  13.8 us (7%)
  other arithmetic  10 us (5%)
    all_gather x1, waiting for transfers between devices, shards(): packed = lax.all_gather(jnp.concatenate(pieces, axis=0), 'col', axis=0)  99.7 us
    dot_general x1, matrix products, shards(): base = jnp.dot(full_rows, weights, preferred_element_type=jnp.float32)  14.7 us
    slice x1, local copies, waits for them, and re-layouts, shards(): weights = packed[:, :bounds[1]].reshape(-1, weight_width)  9.06 us
    all_to_all x1, starting transfers between devices, shards(): lax.all_to_all(jnp.stack([hidden for _ in range(lax.axis_size('row'))], a...  8.27 us
    gather x1, local copies, waits for them, and re-layouts, shards(): jnp.take(key_rotated, rows, axis=0)  6.86 us
    gather x1, local copies, waits for them, and re-layouts, shards(): jnp.take(value_rows, rows, axis=0)  6.86 us
    dot_general x1, matrix products, shards(): jnp.einsum('tf,sfr->tsr', hidden, down_local, preferred_element_type=jnp....  5.55 us
    ppermute x3, starting transfers between devices, shards(): partial = partial + lax.ppermute(partial, 'row', pairs)  5.48 us
  transfers between devices with their start and end apart: 5, of which 1 were waited for; matrix products, arithmetic and copies ran while one was open for 26% of the time, Pallas kernels for 0%

profile of v1, /device:TPU:1, one launch (start us, length us, event | category | flops | bytes accessed | tf_op | source)
XLA Modules:
  0.0 205.9 jit_solution(864731133769735872)
XLA Ops:
  7.2 0.8 reshape.333
  8.0 0.7 reshape.332
  8.8 0.9 copy.32
  9.9 1.8 maximum_bitcast_fusion
  11.7 4.9 %stack.2 = bf16[8,1024,576]{1,2,0:T(8,128)(2,1)} broadcast(bf16[1024,576]{0,1:T(8,128)(2,1)S(1)} %copy-done.3), dimensions={1,2} | broadcast | bytes 10616832 | tf_op jit(solution)/shard_map/gathers/stack | solution.py:87
  16.6 8.3 %all-to-all-start = ((bf16[8,1024,576]{1,2,0:T(8,128)(2,1)}), bf16[8,1024,576]{1,2,0:T(8,128)(2,1)}, u32[]{:S(2)}, u32[]{:S(2)}) async-start(bf16[8,1024,576]{1,2,0:T(8,128)(2,1)} %stack.2), calls=%async_computation | async-start | bytes 18874368 | tf_op jit(solution)/shard_map/gathers/all_to_all | solution.py:86
  25.2 0.7 gather_fusion
  26.2 0.7 compare_and_fusion
  27.0 0.7 fusion.10
  27.6 1.0 multiply_cosine_fusion
  28.6 99.7 %all-gather.4.cloned.1.call-done = bf16[32,174,1024]{2,1,0:T(8,128)(2,1)} async-done(((bf16[1,174,1024]{2,1,0:T(8,128)(2,1)}), bf16[32,174,1024]{2,1,0:T(8,128)(2,1)}) %all-gather.4.cloned.1.call-update) | async-done | bytes 11403280 | tf_op jit(solution)/shard_map/gathers/all_gather | solution.py:103
  128.3 1.4 slice-done.3
  129.7 4.7 %reshape.338 = bf16[32,576,32]{2,1,0:T(8,128)(2,1)} reshape(bf16[32,18,1024]{2,1,0:T(8,128)(2,1)S(1)} %slice-done.3) | data formatting | bytes 2359296 | tf_op jit(solution)/shard_map/gathers/reshape | solution.py:105
  134.5 5.6 %fusion = f32[1024,32]{0,1:T(8,128)S(1)} fusion(bf16[32,576,32]{2,1,0:T(8,128)(2,1)} %reshape.338, pred[1024,32]{0,1:T(8,128)(4,1)S(1)} %get-tuple-element.23, bf16[1024,576]{0,1:T(8,128)(2,1)S(1)} %copy-done.3), kind=kOutput, calls=%fused_computation.4 | convolution fusion | flops 1210023936 | bytes 2523136 | tf_op jit(solution)/shard_map/lowrank/tf,sfr->tsr/dot_general | solution.py:110
  140.0 1.5 collective-permute-start
  141.5 0.6 fusion.4
  142.2 9.1 %slice.58 = bf16[32,144,1024]{2,1,0:T(8,128)(2,1)} slice(bf16[32,174,1024]{2,1,0:T(8,128)(2,1)} %all-gather.4.cloned.1.call-done), slice={[0:32], [0:144], [0:1024]} | slice | bytes 18874368 | tf_op jit(solution)/shard_map/gathers/slice | solution.py:104
  151.3 1.3 collective-permute-start.1
  152.6 14.7 %convolution_bitcast_fusion = f32[1024,1024]{0,1:T(8,128)S(1)} fusion(bf16[4608,1024]{1,0:T(8,128)(2,1)} %bitcast.66, bf16[1024,4608]{0,1:T(8,128)(2,1)} %bitcast.3), kind=kOutput, calls=%fused_computation.5 | convolution fusion | flops 9663676416 | bytes 23068672 | tf_op jit(solution)/shard_map/projection/dot_general | solution.py:138
  167.4 2.7 %collective-permute-start.2 = (f32[1024,32]{0,1:T(8,128)S(1)}, f32[1024,32]{0,1:T(8,128)S(1)}, u32[]{:S(2)}, u32[]{:S(2)}) collective-permute-start(f32[1024,32]{0,1:T(8,128)S(1)} %add.98), channel_id=1, source_target_pairs={{0,128},{32,160},{64,192},{96,224},{128,0},{160,32},{192,64},{224,... | collective-permute-start | bytes 393224 | tf_op jit(solution)/shard_map/lowrank/ppermute | solution.py:117
  170.7 1.4 slice.62
  172.1 1.0 reshape.339
  173.1 0.2 copy.41
  173.3 6.9 %gather_fusion.1 = bf16[2304,256]{1,0:T(8,128)(2,1)S(1)} fusion(bf16[1024,256]{1,0:T(8,128)(2,1)S(1)} %copy.41, s32[3072]{0:T(1024)S(1)} %pad_clamp_fusion), kind=kCustom, calls=%fused_computation.clone | custom fusion | bytes 2368512 | tf_op jit(solution)/shard_map/cache_write/jit(_take)/gather | solution.py:156
  180.2 1.0 broadcast_multiply_fusion
  181.2 2.5 %fusion.1 = bf16[1024,256]{0,1:T(8,128)(2,1)} fusion(bf16[1024,512]{0,1:T(8,128)(2,1)S(1)} %bitcast.71, bf16[512,256]{1,0:T(8,128)(2,1)S(1)} %reshape.343, f32[1024,1024]{0,1:T(8,128)} %copy-done.2), kind=kOutput, calls=%fused_computation.8 | convolution fusion | flops 268959744 | bytes 2883584 | tf_op jit(solution)/shard_map/lowrank/dot_general | solution.py:132
  183.7 1.2 copy.37
  185.0 2.5 %slice_add_fusion = f32[1024,512]{0,1:T(8,128)S(1)} fusion(f32[1024,1024]{0,1:T(8,128)} %copy-done.2, bf16[1024,512]{0,1:T(8,128)(2,1)S(1)} %bitcast.70, bf16[512,512]{1,0:T(8,128)(2,1)} %reshape.339), kind=kOutput, calls=%fused_computation.6 | convolution fusion | flops 537395200 | bytes 5767168 | tf_op jit(solution)/shard_map/lowrank/dot_general | solution.py:127
  187.5 0.3 subtract_convert_fusion
  187.9 1.3 copy.40
  189.3 6.9 %gather_fusion.2 = bf16[2304,256]{1,0:T(8,128)(2,1)S(1)} fusion(bf16[1024,256]{1,0:T(8,128)(2,1)S(1)} %copy.37, s32[3072]{0:T(1024)S(1)} %pad_clamp_fusion), kind=kCustom, calls=%fused_computation.1.clone | custom fusion | bytes 2368512 | tf_op jit(solution)/shard_map/cache_write/jit(_take)/gather | solution.py:159
  196.2 2.9 %select_select_fusion = (bf16[2304,256]{1,0:T(8,128)(2,1)}, bf16[2304,256]{1,0:T(8,128)(2,1)}) fusion(bf16[2304,256]{1,0:T(8,128)(2,1)S(1)} %gather_fusion.2, pred[2304]{0:T(1024)(128)(4,1)S(1)} %copy-done.4, pred[2304]{0:T(1024)(128)(4,1)S(1)} %copy-done.5, bf16[2304,256]{1,0:T(8,128)(2,1)S(1)} %gather_fusion.1), kind=kLoop, calls=%fused_computation.10 | loop fusion | flops 2359296 | bytes 4723200 | tf_op jit(solution)/shard_map/cache_write/jit(_where)/select_n | solution.py:159
  (57 shorter events, 1.8 us)
Async XLA Ops:
  7.2 18.1 %copy-start = (s32[32]{0:T(128)S(1)}, s32[32]{0:T(128)}, u32[]{:S(2)}) copy-start(s32[32]{0:T(128)} %param.22) | copy-start | bytes 388
  7.2 4.5 %copy-start.3 = (bf16[1024,576]{0,1:T(8,128)(2,1)S(1)}, bf16[1024,576]{0,1:T(8,128)(2,1)}, u32[]{:S(2)}) copy-start(bf16[1024,576]{0,1:T(8,128)(2,1)} %param.13) | copy-start | bytes 3538948
  7.2 121.1 %all-gather.4.cloned.1.call-start = ((), (), s32[]{:S(2)}) async-start(), calls=%async_computation.1 | async-start | bytes 11894784 | tf_op jit(solution)/shard_map/gathers/all_gather | solution.py:103
  16.5 8.3 %copy-start.6 = (s32[1,10]{1,0:T(1,128)S(1)}, s32[1,10]{1,0:T(1,128)}, u32[]{:S(2)}) copy-start(s32[1,10]{1,0:T(1,128)} %param.20) | copy-start | bytes 124
  16.5 8.7 %copy-start.7 = (s32[1,10]{1,0:T(1,128)S(1)}, s32[1,10]{1,0:T(1,128)}, u32[]{:S(2)}) copy-start(s32[1,10]{1,0:T(1,128)} %param.21) | copy-start | bytes 124
  16.6 9.4 %copy-start.8 = (s32[1,18]{1,0:T(1,128)S(1)}, s32[1,18]{1,0:T(1,128)}, u32[]{:S(2)}) copy-start(s32[1,18]{1,0:T(1,128)} %param.23) | copy-start | bytes 220
  16.6 136.0 %all-to-all-start = ((bf16[8,1024,576]{1,2,0:T(8,128)(2,1)}), bf16[8,1024,576]{1,2,0:T(8,128)(2,1)}, u32[]{:S(2)}, u32[]{:S(2)}) async-start(bf16[8,1024,576]{1,2,0:T(8,128)(2,1)} %stack.2), calls=%async_computation | async-start | bytes 18874368 | tf_op jit(solution)/shard_map/gathers/all_to_all | solution.py:86
  128.3 1.4 slice-start.3
  140.0 11.2 %collective-permute-start = (f32[1024,32]{0,1:T(8,128)S(1)}, f32[1024,32]{0,1:T(8,128)S(1)}, u32[]{:S(2)}, u32[]{:S(2)}) collective-permute-start(f32[1024,32]{0,1:T(8,128)S(1)} %fusion), channel_id=1, source_target_pairs={{0,32},{32,0},{64,96},{96,64},{128,160},{160,128},{192,224},{224,1... | collective-permute-start | bytes 393224 | tf_op jit(solution)/shard_map/lowrank/ppermute | solution.py:117
  151.3 16.1 %collective-permute-start.1 = (f32[1024,32]{0,1:T(8,128)S(1)}, f32[1024,32]{0,1:T(8,128)S(1)}, u32[]{:S(2)}, u32[]{:S(2)}) collective-permute-start(f32[1024,32]{0,1:T(8,128)S(1)} %add.97), channel_id=1, source_target_pairs={{0,64},{32,96},{64,0},{96,32},{128,192},{160,224},{192,128},{224,1... | collective-permute-start | bytes 393224 | tf_op jit(solution)/shard_map/lowrank/ppermute | solution.py:117
  152.6 17.7 %slice-start = ((s8[11534336]{0:T(1024)(128)(4,1)}), s8[4194304]{0:T(1024)(128)(4,1)S(1)}, s32[]{:S(2)}) async-start(s8[11534336]{0:T(1024)(128)(4,1)} %bitcast.64), calls=%async_computation.2 | async-start | bytes 8388608
  152.6 17.8 %slice-start.1 = ((s8[11534336]{0:T(1024)(128)(4,1)}), s8[4194304]{0:T(1024)(128)(4,1)S(1)}, s32[]{:S(2)}) async-start(s8[11534336]{0:T(1024)(128)(4,1)} %bitcast.64), calls=%async_computation.3 | async-start | bytes 8388608
  152.6 17.8 %slice-start.2 = ((s8[11534336]{0:T(1024)(128)(4,1)}), s8[3145728]{0:T(1024)(128)(4,1)S(1)}, s32[]{:S(2)}) async-start(s8[11534336]{0:T(1024)(128)(4,1)} %bitcast.64), calls=%async_computation.4 | async-start | bytes 6291456
  167.3 3.0 %copy-start.2 = (f32[1024,1024]{0,1:T(8,128)}, f32[1024,1024]{0,1:T(8,128)S(1)}, u32[]{:S(2)}) copy-start(f32[1024,1024]{0,1:T(8,128)S(1)} %convolution_bitcast_fusion) | copy-start | bytes 12582916
  167.4 12.8 %collective-permute-start.2 = (f32[1024,32]{0,1:T(8,128)S(1)}, f32[1024,32]{0,1:T(8,128)S(1)}, u32[]{:S(2)}, u32[]{:S(2)}) collective-permute-start(f32[1024,32]{0,1:T(8,128)S(1)} %add.98), channel_id=1, source_target_pairs={{0,128},{32,160},{64,192},{96,224},{128,0},{160,32},{192,64},{224,... | collective-permute-start | bytes 393224 | tf_op jit(solution)/shard_map/lowrank/ppermute | solution.py:117
  189.3 6.9 %copy-start.4 = (pred[2304]{0:T(1024)(128)(4,1)S(1)}, pred[2304]{0:T(1024)(128)(4,1)}, u32[]{:S(2)}) copy-start(pred[2304]{0:T(1024)(128)(4,1)} %compare_and_fusion) | copy-start | bytes 6916
  189.3 6.9 %copy-start.5 = (pred[2304]{0:T(1024)(128)(4,1)S(1)}, pred[2304]{0:T(1024)(128)(4,1)}, u32[]{:S(2)}) copy-start(pred[2304]{0:T(1024)(128)(4,1)} %fusion.4) | copy-start | bytes 6916
  189.3 9.8 %copy-start.1 = (s32[32]{0:T(128)S(1)}, s32[32]{0:T(128)}, u32[]{:S(2)}) copy-start(s32[32]{0:T(128)} %param.22) | copy-start | bytes 388
Sparse Core Ops, SparseCore 0:
  11.8 116.4 all-gather.3
